TPU v7x, 256 devices: a whole 4x4x8 slice. The times are simulated.
256 devices in a mesh: section: 2 (over core), req: 32 (over z, y), head: 4 (over x).
Axes of the slice: x: 4, y: 4, z: 8, core: 2. Of those that a mesh axis runs over, the one named last changes fastest.
Arguments:
- token_ids: int32 [128, 4], P('req'), may hold values from 0 to 31999
- request_order: int32 [128], replicated, may hold values from 0 to 127, each once
- window_lengths: int32 [128], replicated, may hold values from 1 to 512, as said below
- embed_table: bfloat16 [32000, 2048], P(('req', 'head')), may hold values from -6 to 6
- cache_arrived: bfloat16 [2, 128, 512, 2, 2048], P('section', None, 'req', None, 'head'), may hold values from -16 to 16
- state_arrived: float32 [2, 128, 128, 16, 128], P('section', None, 'req', 'head'), may hold values from -2 to 2
- conv_history: bfloat16 [2, 128, 3, 3, 2048], P('section', 'req', None, None, 'head'), may hold values from -6 to 6
- sink_cache: bfloat16 [2, 128, 4, 2, 2048], P('section', 'req', None, None, 'head'), may hold values from -16 to 16
- w_qkv: bfloat16 [2, 2048, 3, 2048], P('section', None, None, 'head'), may hold values from -0.125 to 0.125
- w_out: bfloat16 [2, 2048, 2048], P('section', 'head'), may hold values from -0.125 to 0.125
- w_beta: bfloat16 [2, 2048, 16], P('section', None, 'head'), may hold values from -0.125 to 0.125
- conv_taps: float32 [2, 4, 3, 2048], P('section', None, None, 'head'), may hold values from -3 to 3
- pre_gain: float32 [2, 2048], P('section'), may hold values from 0.25 to 1.75
- out_gain: float32 [2, 2048], P('section', 'head'), may hold values from 0.25 to 1.75
- score_scale_table: float32 [2, 16], P('section', 'head'), may hold values from 4 to 512
Outputs:
- layer_out: bfloat16 [2, 128, 4, 2048], P('section', 'req')
- final_state: float32 [2, 128, 128, 16, 128], P('section', 'req', None, 'head')
Inputs may be any that keep to these rules, and one draw needn't show every extreme that they name: `request_order`: a permutation of the arriving requests. `window_lengths`: some request holds a full window.
All inputs are finite; a program needn't handle non-finite values.
Results may differ from a plain program's by a relative error of at most 0.025.
Values may be sent and summed in bfloat16 or wider, within the bound.
No kernel may reach another device: no remote copies, remote signals or barrier semaphores. Data moves between devices by JAX's collectives and lax.ppermute only.
A program may use at most 128 MiB of HBM per device.

v0:
```python
import jax
import jax.numpy as jnp
from jax import lax
from jax.sharding import PartitionSpec as P

WIN = 512
epsilon = 1e-06
negative_big = -1e30


def passed_along(value, axis, by):
    peers = lax.axis_size(axis)
    pairs = [(i, i + by) for i in range(peers) if 0 <= i + by < peers]
    return lax.ppermute(value, axis, pairs)


def rms_scale(values, gain_row):
    return (
        values * lax.rsqrt(jnp.mean(values * values, axis=-1, keepdims=True) + epsilon) * gain_row
    )


def unit_rows(values):
    return values * lax.rsqrt(jnp.sum(values * values, axis=-1, keepdims=True) + epsilon)


def shards(
    token_ids,
    request_order,
    window_lengths,
    embed_table,
    cache_arrived,
    state_arrived,
    conv_history,
    sink_cache,
    w_qkv,
    w_out,
    w_beta,
    conv_taps,
    pre_gain,
    out_gain,
    score_scale_table,
):
    slot_count, token_count = token_ids.shape
    heads_dev = score_scale_table.shape[1]
    width = pre_gain.shape[1]
    local_width = out_gain.shape[1]
    head_dim = local_width // heads_dev
    group_index = lax.axis_index("req")
    section_index = lax.axis_index("section")
    vocab_dev = embed_table.shape[0]
    all_ids = lax.all_gather(token_ids, "req", axis=0, tiled=True)
    first_row = lax.axis_index(("req", "head")) * vocab_dev
    onehot = (
        all_ids.reshape(-1)[:, None] == first_row + jnp.arange(vocab_dev, dtype=jnp.int32)[None, :]
    ).astype(jnp.bfloat16)
    looked_up = jnp.dot(onehot, embed_table, preferred_element_type=jnp.float32)
    summed = lax.psum(looked_up, ("req", "head"))
    own_rows = lax.dynamic_slice_in_dim(
        summed, group_index * slot_count * token_count, slot_count * token_count, 0
    )
    embedded = own_rows.astype(jnp.bfloat16).reshape(slot_count, token_count, width)
    ordered_states = jnp.take(state_arrived, request_order, axis=1)
    delta_state = lax.all_to_all(ordered_states, "req", split_axis=1, concat_axis=2, tiled=True)[0]
    ordered_cache = jnp.take(cache_arrived, request_order, axis=1)
    all_lengths = jnp.take(window_lengths, request_order)
    own_lengths = lax.dynamic_slice_in_dim(all_lengths, group_index * slot_count, slot_count, 0)
    window_cache = lax.all_to_all(ordered_cache, "req", split_axis=1, concat_axis=2, tiled=True)[0]
    cache_rows = window_cache.shape[1]
    cache_holders = window_cache.shape[0]
    stored_key_rows = window_cache[:, :, 0].reshape(cache_holders, cache_rows, heads_dev, head_dim)
    cache_values = window_cache[:, :, 1].reshape(cache_holders, cache_rows, heads_dev, head_dim)
    sink_count = sink_cache.shape[2]
    anchor_key_rows = sink_cache[0][:, :, 0].reshape(slot_count, sink_count, heads_dev, head_dim)
    sink_values = sink_cache[0][:, :, 1].reshape(slot_count, sink_count, heads_dev, head_dim)
    qkv_matrix = w_qkv[0].reshape(width, 3 * local_width)
    conv_weights = conv_taps[0]
    softmax_scale_factor = score_scale_table[0]
    gain_head = out_gain[0].reshape(heads_dev, head_dim)
    new_index = jnp.arange(token_count, dtype=jnp.int32)
    row_index = jnp.arange(cache_rows, dtype=jnp.int32)
    history = conv_history[0]
    new_keys = jnp.zeros((slot_count, token_count, heads_dev, head_dim), jnp.bfloat16)
    new_values = jnp.zeros((slot_count, token_count, heads_dev, head_dim), jnp.bfloat16)
    received = jnp.zeros((slot_count, width), jnp.bfloat16)
    produced = jnp.zeros((slot_count, token_count, width), jnp.bfloat16)
    for position in range(token_count + 1):
        t_raw = position - section_index
        is_valid = (t_raw >= 0) & (t_raw < token_count)
        t_index = jnp.clip(t_raw, 0, token_count - 1)
        fresh_input = embedded[:, min(position, token_count - 1)]
        stream_in = jnp.where(section_index == 0, fresh_input, received)
        mixer_history = history
        mixer_delta_state = delta_state
        mixer_new_keys = new_keys
        mixer_new_values = new_values
        normed = rms_scale(stream_in.astype(jnp.float32), pre_gain[0]).astype(jnp.bfloat16)
        projected = (
            jnp.dot(normed, qkv_matrix, preferred_element_type=jnp.float32)
            .astype(jnp.bfloat16)
            .reshape(slot_count, 3, local_width)
        )
        conv_window = jnp.concatenate([mixer_history, projected[:, None]], axis=1)
        activated = jax.nn.silu(
            jnp.sum(conv_window.astype(jnp.float32) * conv_weights[None], axis=1)
        )
        query_vec = unit_rows(activated[:, 0].reshape(slot_count, heads_dev, head_dim))
        key_vec = unit_rows(activated[:, 1].reshape(slot_count, heads_dev, head_dim))
        value_vec = activated[:, 2].reshape(slot_count, heads_dev, head_dim)
        beta_gate = jax.nn.sigmoid(jnp.dot(normed, w_beta[0], preferred_element_type=jnp.float32))
        predicted = jnp.einsum(
            "skhv,shk->shv", mixer_delta_state, key_vec, precision=lax.Precision.HIGHEST
        )
        update = jnp.transpose(key_vec, (0, 2, 1))[:, :, :, None] * (value_vec - predicted)[:, None]
        mixer_delta_state = mixer_delta_state + beta_gate[:, None, :, None] * update
        readout = jnp.einsum(
            "skhv,shk->shv", mixer_delta_state, query_vec, precision=lax.Precision.HIGHEST
        )
        query_halfwidth = query_vec.astype(jnp.bfloat16)
        mixer_new_keys = lax.dynamic_update_slice_in_dim(
            mixer_new_keys, key_vec.astype(jnp.bfloat16)[:, None], t_index, 1
        )
        mixer_new_values = lax.dynamic_update_slice_in_dim(
            mixer_new_values, value_vec.astype(jnp.bfloat16)[:, None], t_index, 1
        )
        anchor_score_rows = (
            jnp.einsum(
                "kry,kgry->krg",
                query_halfwidth,
                anchor_key_rows,
                preferred_element_type=jnp.float32,
            )
            * softmax_scale_factor[None, :, None]
        )
        incoming_score_rows = (
            jnp.einsum(
                "kry,kgry->krg", query_halfwidth, mixer_new_keys, preferred_element_type=jnp.float32
            )
            * softmax_scale_factor[None, :, None]
        )
        fresh_mask = (new_index <= t_index)[None, None, :]
        home_max = jnp.maximum(
            jnp.max(anchor_score_rows, axis=-1),
            jnp.max(jnp.where(fresh_mask, incoming_score_rows, negative_big), axis=-1),
        )
        limit = jnp.maximum(WIN - own_lengths, t_index + 1)
        cache_mask = row_index[None, None, :] >= limit[:, None, None]
        stored_score_rows = (
            jnp.einsum(
                "xqa,xeqa->xqe",
                query_halfwidth,
                stored_key_rows,
                preferred_element_type=jnp.float32,
            )
            * softmax_scale_factor[None, :, None]
        )
        highest = jnp.maximum(
            home_max, jnp.max(jnp.where(cache_mask, stored_score_rows, negative_big), axis=-1)
        )
        cache_weights = jnp.where(cache_mask, jnp.exp(stored_score_rows - highest[:, :, None]), 0.0)
        cache_sum = jnp.sum(cache_weights, axis=-1)
        cache_part = jnp.einsum(
            "shw,swhd->shd",
            cache_weights.astype(jnp.bfloat16),
            cache_values,
            preferred_element_type=jnp.float32,
        )
        sink_weights = jnp.exp(anchor_score_rows - highest[:, :, None])
        fresh_weights = jnp.where(
            fresh_mask, jnp.exp(incoming_score_rows - highest[:, :, None]), 0.0
        )
        weight_sum = cache_sum + jnp.sum(sink_weights, axis=-1) + jnp.sum(fresh_weights, axis=-1)
        numerator = cache_part + jnp.einsum(
            "shj,sjhd->shd",
            sink_weights.astype(jnp.bfloat16),
            sink_values,
            preferred_element_type=jnp.float32,
        )
        numerator = numerator + jnp.einsum(
            "shj,sjhd->shd",
            fresh_weights.astype(jnp.bfloat16),
            mixer_new_values,
            preferred_element_type=jnp.float32,
        )
        attended = numerator / weight_sum[:, :, None]
        mixed_heads = (
            (rms_scale(readout, gain_head[None]) + attended)
            .astype(jnp.bfloat16)
            .reshape(slot_count, local_width)
        )
        partial_out = jnp.dot(mixed_heads, w_out[0], preferred_element_type=jnp.float32)
        mixer_out = lax.psum(partial_out, "head")
        stream_out = (stream_in.astype(jnp.float32) + mixer_out).astype(jnp.bfloat16)
        mixer_history = jnp.concatenate([mixer_history[:, 1:], projected[:, None]], axis=1)
        stream_out, next_history, next_state, next_keys, next_values = (
            stream_out,
            mixer_history,
            mixer_delta_state,
            mixer_new_keys,
            mixer_new_values,
        )
        history = jnp.where(is_valid, next_history, history)
        delta_state = jnp.where(is_valid, next_state, delta_state)
        new_keys = jnp.where(is_valid, next_keys, new_keys)
        new_values = jnp.where(is_valid, next_values, new_values)
        stored = lax.dynamic_update_slice_in_dim(produced, stream_out[:, None], t_index, 1)
        produced = jnp.where(is_valid, stored, produced)
        if position < token_count:
            received = passed_along(stream_out, "section", 1)
    return (produced[None], delta_state[None])


def solution(mesh):
    return jax.shard_map(
        shards,
        mesh=mesh,
        in_specs=(
            P("req", None),
            P(),
            P(),
            P(("req", "head"), None),
            P("section", None, "req", None, "head"),
            P("section", None, "req", "head", None),
            P("section", "req", None, None, "head"),
            P("section", "req", None, None, "head"),
            P("section", None, None, "head"),
            P("section", "head", None),
            P("section", None, "head"),
            P("section", None, None, "head"),
            P("section", None),
            P("section", "head"),
            P("section", "head"),
        ),
        out_specs=(P("section", "req", None, None), P("section", "req", None, "head", None)),
        check_vma=False,
    )
```

profile of v0, /device:TPU:2, one launch (start us, length us, event | category | flops | bytes accessed | tf_op | source)
XLA Modules:
  0.0 1202.1 jit_solution(7097759639940147544)
XLA Ops:
  3.7 2.4 gather_fusion
  7.4 11.5 all-to-all-start
  18.9 66.6 %all-gather = s32[32,4,4]{2,1,0:T(4,128)S(1)} all-gather(s32[1,4,4]{2,1,0:T(4,128)S(1)} %bitcast.617), channel_id=1, replica_groups=mesh['section'=2,'req'=32,'head'=4] {'req'}, dimensions={0}, use_global_device_ids=true | all-gather | bytes 2112 | tf_op jit(solution)/shard_map/all_gather | solution.py:52
  85.6 4.1 fusion.75
  89.7 3.2 copy.413
  92.9 5.1 gather_fusion.2
  98.0 4.7 fusion
  103.7 8.2 all-to-all-start.1
  111.9 792.8 %all-reduce.1 = bf16[512,2048]{1,0:T(8,128)(2,1)} all-reduce(f32[512,2048]{1,0:T(8,128)} %fusion.75), channel_id=1, replica_groups=mesh['section'=2,'req'=32,'head'=4] {'req','head'}, use_global_device_ids=true, to_apply=%region_0.0 | all-reduce | flops 1048576 | bytes 6291456 | tf_op jit(solution)/shard_map/psum | solution.py:58
  905.6 8.8 copy.140
  915.4 4.5 convolution_convert_fusion.4
  929.7 2.7 copy.144
  932.4 2.5 fusion.279
  934.9 4.2 copy.145
  941.5 4.2 copy.146
  945.8 2.2 fusion.114
  948.7 20.5 %psum.43 = f32[4,2048]{1,0:T(4,128)S(1)} all-reduce(f32[4,2048]{1,0:T(4,128)S(1)} %fusion.9), channel_id=1, replica_groups=mesh['section'=2,'req'=32,'head'=4] {'head'}, use_global_device_ids=true, to_apply=%region_12.13 | all-reduce | flops 8192 | bytes 65536 | tf_op jit(solution)/shard_map/psum | solution.py:192
  978.5 4.5 convolution_convert_fusion.3
  1005.6 15.6 %psum.44 = f32[4,2048]{1,0:T(4,128)} all-reduce(f32[4,2048]{1,0:T(4,128)} %fusion.7), channel_id=1, replica_groups=mesh['section'=2,'req'=32,'head'=4] {'head'}, use_global_device_ids=true, to_apply=%region_24.25 | all-reduce | flops 8192 | bytes 65536 | tf_op jit(solution)/shard_map/psum | solution.py:192
  1033.1 4.5 convolution_convert_fusion.2
  1055.3 2.2 fusion.271
  1057.8 2.7 fusion.33
  1062.5 16.8 %psum.45 = f32[4,2048]{1,0:T(4,128)} all-reduce(f32[4,2048]{1,0:T(4,128)S(1)} %fusion.5), channel_id=1, replica_groups=mesh['section'=2,'req'=32,'head'=4] {'head'}, use_global_device_ids=true, to_apply=%region_36.37 | all-reduce | flops 8192 | bytes 65536 | tf_op jit(solution)/shard_map/psum | solution.py:192
  1092.9 4.5 convolution_convert_fusion.1
  1112.9 2.5 fusion.80
  1115.6 3.4 fusion.31
  1121.9 15.6 %psum.46 = f32[4,2048]{1,0:T(4,128)} all-reduce(f32[4,2048]{1,0:T(4,128)} %fusion.3), channel_id=1, replica_groups=mesh['section'=2,'req'=32,'head'=4] {'head'}, use_global_device_ids=true, to_apply=%region_48.49 | all-reduce | flops 8192 | bytes 65536 | tf_op jit(solution)/shard_map/psum | solution.py:192
  1146.6 4.5 convolution_convert_fusion
  1166.7 3.6 fusion.39
  1172.0 3.4 fusion.26
  1177.1 16.8 %psum.47 = f32[4,2048]{1,0:T(4,128)} all-reduce(f32[4,2048]{1,0:T(4,128)S(1)} %fusion.1), channel_id=1, replica_groups=mesh['section'=2,'req'=32,'head'=4] {'head'}, use_global_device_ids=true, to_apply=%region_60.61 | all-reduce | flops 8192 | bytes 65536 | tf_op jit(solution)/shard_map/psum | solution.py:192
  1196.8 5.1 add_select_fusion
  (507 shorter events, 145.6 us)
Async XLA Ops:
  0.6 947.7 %copy-start = (bf16[1,512,2048]{2,1,0:T(8,128)(2,1)S(1)}, bf16[1,512,2048]{2,1,0:T(8,128)(2,1)}, u32[]{:S(2)}) copy-start(bf16[1,512,2048]{2,1,0:T(8,128)(2,1)} %param.24) | copy-start | bytes 6291460
  6.1 12.8 %copy-start.117 = (s32[4,4]{1,0:T(4,128)S(1)}, s32[4,4]{1,0:T(4,128)}, u32[]{:S(2)}) copy-start(s32[4,4]{1,0:T(4,128)} %param.15) | copy-start | bytes 196
  7.4 95.3 %all-to-all-start = ((f32[1,128,4,4,128]{4,3,2,0,1:T(4,128)}), f32[1,128,4,4,128]{4,3,2,0,1:T(4,128)S(1)}, u32[]{:S(2)}, u32[]{:S(2)}) async-start(f32[1,128,4,4,128]{4,3,2,0,1:T(4,128)} %bitcast_select_fusion.1), calls=%async_computation | async-start | bytes 2097152 | tf_op jit(solution)/shard_map/all_to_all | solution.py:64
  103.7 826.0 %all-to-all-start.1 = ((bf16[1,128,16,2,512]{4,2,3,0,1:T(8,128)(2,1)}), bf16[1,128,16,2,512]{4,2,3,0,1:T(8,128)(2,1)}, u32[]{:S(2)}, u32[]{:S(2)}) async-start(bf16[1,128,16,2,512]{4,2,3,0,1:T(8,128)(2,1)} %fusion), calls=%async_computation.1 | async-start | bytes 8388608 | tf_op jit(solution)/shard_map/all_to_all | solution.py:68
  111.8 792.8 %copy-start.11 = (bf16[1,4,3,3,512]{4,1,3,2,0:T(4,128)(2,1)S(1)}, bf16[1,4,3,3,512]{4,1,3,2,0:T(4,128)(2,1)}, u32[]{:S(2)}) copy-start(bf16[1,4,3,3,512]{4,1,3,2,0:T(4,128)(2,1)} %param.21) | copy-start | bytes 110596
  111.8 792.8 %copy-start.80 = (f32[1,4,3,512]{3,1,2,0:T(4,128)S(1)}, f32[1,4,3,512]{3,1,2,0:T(4,128)}, u32[]{:S(2)}) copy-start(f32[1,4,3,512]{3,1,2,0:T(4,128)} %param.26) | copy-start | bytes 73732
  905.6 9.7 copy-start.12
  915.3 9.7 copy-start.118
  922.2 7.4 copy-start.92
  922.2 25.9 %copy-start.87 = (bf16[4,4,512]{2,1,0:T(4,128)(2,1)}, bf16[4,4,512]{2,1,0:T(4,128)(2,1)S(1)}, u32[]{:S(2)}) copy-start(bf16[4,4,512]{2,1,0:T(4,128)(2,1)S(1)} %get-tuple-element.16) | copy-start | bytes 49156
  925.9 57.2 %copy-start.8 = (bf16[4,3,3,512]{3,0,2,1:T(4,128)(2,1)}, bf16[4,3,3,512]{3,0,2,1:T(4,128)(2,1)S(1)}, u32[]{:S(2)}) copy-start(bf16[4,3,3,512]{3,0,2,1:T(4,128)(2,1)S(1)} %maximum_select_fusion) | copy-start | bytes 110596
  969.9 7.7 collective-permute-start
  984.3 16.2 %copy-start.30 = (f32[4,4,128]{2,1,0:T(4,128)S(1)}, f32[4,4,128]{2,1,0:T(4,128)}, u32[]{:S(2)}) copy-start(f32[4,4,128]{2,1,0:T(4,128)} %copy-done.29) | copy-start | bytes 24580
  984.3 16.2 %copy-start.35 = (f32[4,128,4]{1,2,0:T(4,128)S(1)}, f32[4,128,4]{1,2,0:T(4,128)}, u32[]{:S(2)}) copy-start(f32[4,128,4]{1,2,0:T(4,128)} %copy-done.34) | copy-start | bytes 24580
  985.1 17.6 %copy-start.64 = (f32[4,128,4]{1,2,0:T(4,128)}, f32[4,128,4]{1,2,0:T(4,128)S(1)}, u32[]{:S(2)}) copy-start(f32[4,128,4]{1,2,0:T(4,128)S(1)} %fusion.317) | copy-start | bytes 24580
  987.3 9.8 copy-start.79
  1002.9 18.3 %slice-start = ((bf16[4,3,3,512]{3,0,2,1:T(4,128)(2,1)}), bf16[4,2,3,512]{3,0,2,1:T(4,128)(2,1)S(1)}, s32[]{:S(2)}) async-start(bf16[4,3,3,512]{3,0,2,1:T(4,128)(2,1)} %copy-done.8), calls=%async_computation.2 | async-start | bytes 49152 | tf_op jit(solution)/shard_map/slice | solution.py:194
  1002.9 18.3 %copy-start.25 = (bf16[4,1536]{1,0:T(4,128)(2,1)S(1)}, bf16[4,1536]{1,0:T(4,128)(2,1)}, u32[]{:S(2)}) copy-start(bf16[4,1536]{1,0:T(4,128)(2,1)} %copy-done.24) | copy-start | bytes 36868
  1023.2 7.5 collective-permute-start.1
  1026.6 11.1 copy-start.21
  1037.7 17.7 %copy-start.31 = (f32[4,4,128]{2,1,0:T(4,128)S(1)}, f32[4,4,128]{2,1,0:T(4,128)}, u32[]{:S(2)}) copy-start(f32[4,4,128]{2,1,0:T(4,128)} %copy-done.29) | copy-start | bytes 24580
  1046.1 11.5 copy-start.36
  1080.1 17.3 %copy-start.9 = (bf16[4,3,3,512]{3,0,2,1:T(4,128)(2,1)}, bf16[4,3,3,512]{3,0,2,1:T(4,128)(2,1)S(1)}, u32[]{:S(2)}) copy-start(bf16[4,3,3,512]{3,0,2,1:T(4,128)(2,1)S(1)} %maximum_select_fusion.2) | copy-start | bytes 110596
  1081.5 8.9 collective-permute-start.2
  1119.2 18.3 %slice-start.1 = ((bf16[4,3,3,512]{3,0,2,1:T(4,128)(2,1)}), bf16[4,2,3,512]{3,0,2,1:T(4,128)(2,1)S(1)}, s32[]{:S(2)}) async-start(bf16[4,3,3,512]{3,0,2,1:T(4,128)(2,1)} %copy-done.9), calls=%async_computation.3 | async-start | bytes 49152 | tf_op jit(solution)/shard_map/slice | solution.py:194
  1119.2 18.3 %copy-start.27 = (bf16[4,1536]{1,0:T(4,128)(2,1)S(1)}, bf16[4,1536]{1,0:T(4,128)(2,1)}, u32[]{:S(2)}) copy-start(bf16[4,1536]{1,0:T(4,128)(2,1)} %copy-done.26) | copy-start | bytes 36868
  1139.0 6.7 collective-permute-start.3
  1151.1 9.4 copy-start.81
  1156.2 9.9 copy-start.78
  1175.7 21.1 %copy-start.5 = (f32[1,4,32,4,4,128]{5,4,3,2,1,0:T(4,128)S(1)}, f32[1,4,32,4,4,128]{5,4,3,2,1,0:T(4,128)}, u32[]{:S(2)}) copy-start(f32[1,4,32,4,4,128]{5,4,3,2,1,0:T(4,128)} %copy.150) | copy-start | bytes 3145732
  1176.4 20.4 %copy-start.59 = (f32[4,4,128]{2,1,0:T(4,128)S(1)}, f32[4,4,128]{2,1,0:T(4,128)}, u32[]{:S(2)}) copy-start(f32[4,4,128]{2,1,0:T(4,128)} %copy-done.56) | copy-start | bytes 24580
  1176.4 20.4 %copy-start.62 = (f32[4,4,128]{2,1,0:T(4,128)S(1)}, f32[4,4,128]{2,1,0:T(4,128)}, u32[]{:S(2)}) copy-start(f32[4,4,128]{2,1,0:T(4,128)} %copy-done.60) | copy-start | bytes 24580
  (97 other events, 306.7 us)
where the time goes:
time: 1210 us; the launch traced here: 1200 us
  blocking collectives  945 us (78%)
  matrix products  81.3 us (7%)
  local copies, waits for them, and re-layouts  76.8 us (6%)
  other arithmetic  69.3 us (6%)
  starting transfers between devices  27.5 us (2%)
    psum x1, blocking collectives, shards(): summed = lax.psum(looked_up, ('req', 'head'))  793 us
    psum x5, blocking collectives, shards(): mixer_out = lax.psum(partial_out, 'head')  85.3 us
    all_gather x1, blocking collectives, shards(): all_ids = lax.all_gather(token_ids, 'req', axis=0, tiled=True)  66.6 us
  transfers between devices with their start and end apart: 6, of which 0 were waited for; matrix products, arithmetic and copies ran while one was open for 5% of the time, Pallas kernels for 0%

commit v1 on v0

--- a/solution.py
+++ b/solution.py
@@ -55,7 +55,7 @@
         all_ids.reshape(-1)[:, None] == first_row + jnp.arange(vocab_dev, dtype=jnp.int32)[None, :]
     ).astype(jnp.bfloat16)
     looked_up = jnp.dot(onehot, embed_table, preferred_element_type=jnp.float32)
-    summed = lax.psum(looked_up, ("req", "head"))
+    summed = lax.psum(lax.psum(looked_up, "head"), "req")
     own_rows = lax.dynamic_slice_in_dim(
         summed, group_index * slot_count * token_count, slot_count * token_count, 0
     )

time: 1210 us -> 645 us (0.53)
  blocking collectives: 945 us -> 324 us
  waiting for transfers between devices: 0.02 us -> 41 us
  between operations: 2.47 us -> 15.8 us
    psum x1, blocking collectives: 793 us -> 193 us  [shards(): summed = lax.psum(lax.psum(looked_up, 'head'), 'req')]
    psum x0 -> x1, waiting for transfers between devices: none -> 40.3 us  [shards(): summed = lax.psum(lax.psum(looked_up, 'head'), 'req')]
    all_gather x1, blocking collectives: 66.6 us -> 52.3 us  [shards(): all_ids = lax.all_gather(token_ids, 'req', axis=0, tiled=True)]
    unnamed x252 -> x248, local copies, waits for them, and re-layouts: 23.8 us -> 26.5 us
  transfers between devices with their start and end apart: 6 -> 7, of which waited for: 0 -> 2; matrix products, arithmetic and copies ran while one was open for 5% -> 11% of each run, Pallas kernels for 0% -> 0%
where the time goes in v1:
time: 645 us; the launch traced here: 634 us
  blocking collectives  324 us (50%)
  matrix products  82 us (13%)
  local copies, waits for them, and re-layouts  79.2 us (12%)
  other arithmetic  68.4 us (11%)
  waiting for transfers between devices  41 us (6%)
  starting transfers between devices  23.3 us (4%)
  between operations  15.8 us (2%)
    psum x1, blocking collectives, shards(): summed = lax.psum(lax.psum(looked_up, 'head'), 'req')  193 us
    psum x5, blocking collectives, shards(): mixer_out = lax.psum(partial_out, 'head')  78.8 us
    all_gather x1, blocking collectives, shards(): all_ids = lax.all_gather(token_ids, 'req', axis=0, tiled=True)  52.3 us
    psum x1, waiting for transfers between devices, shards(): summed = lax.psum(lax.psum(looked_up, 'head'), 'req')  40.3 us
    unnamed x248, local copies, waits for them, and re-layouts  26.5 us
    dot_general x5, matrix products, shards(): jnp.dot(normed, qkv_matrix, preferred_element_type=jnp.float32)  22.5 us
    dot_general x5, matrix products, shards(): jnp.einsum('skhv,shk->shv', mixer_delta_state, query_vec, precision=lax.P...  12.9 us
  transfers between devices with their start and end apart: 7, of which 2 were waited for; matrix products, arithmetic and copies ran while one was open for 11% of the time, Pallas kernels for 0%

profile of v1, /device:TPU:2, one launch (start us, length us, event | category | flops | bytes accessed | tf_op | source)
XLA Modules:
  0.0 633.7 jit_solution(8546508393771573547)
XLA Ops:
  7.2 52.3 %all-gather = s32[32,4,4]{2,1,0:T(4,128)S(1)} all-gather(s32[1,4,4]{2,1,0:T(4,128)} %bitcast.617), channel_id=1, replica_groups=mesh['section'=2,'req'=32,'head'=4] {'req'}, dimensions={0}, use_global_device_ids=true | all-gather | bytes 2112 | tf_op jit(solution)/shard_map/all_gather | solution.py:52
  59.6 4.1 fusion.75
  65.6 2.4 gather_fusion
  69.3 6.1 all-to-all-start
  75.5 5.3 copy.413
  80.8 5.1 gather_fusion.2
  88.4 4.7 fusion
  94.7 9.3 %all-to-all-start.1 = ((bf16[1,128,16,2,512]{4,2,3,0,1:T(8,128)(2,1)}), bf16[1,128,16,2,512]{4,2,3,0,1:T(8,128)(2,1)}, u32[]{:S(2)}, u32[]{:S(2)}) async-start(bf16[1,128,16,2,512]{4,2,3,0,1:T(8,128)(2,1)} %fusion), calls=%async_computation.1 | async-start | bytes 8388608 | tf_op jit(solution)/shard_map/all_to_all | solution.py:68
  104.6 8.9 %copy.140 = bf16[1,2048,3,512]{1,3,2,0:T(8,128)(2,1)} copy(bf16[1,2048,3,512]{3,1,2,0:T(8,128)(2,1)} %param.23) | data formatting | bytes 12582912 | tf_op args[8]
  117.9 40.3 %all-reduce.3.cloned.1.call-done = f32[512,2048]{1,0:T(8,128)} async-done(((f32[512,2048]{1,0:T(8,128)}), f32[512,2048]{1,0:T(8,128)}) %all-reduce.3.cloned.1.call-update) | async-done | bytes 4194320 | tf_op jit(solution)/shard_map/psum | solution.py:58
  158.3 193.1 %all-reduce.4 = bf16[512,2048]{1,0:T(8,128)(2,1)} all-reduce(f32[512,2048]{1,0:T(8,128)} %all-reduce.3.cloned.1.call-done), channel_id=1, replica_groups=mesh['section'=2,'req'=32,'head'=4] {'req'}, use_global_device_ids=true, to_apply=%region_1.0 | all-reduce | flops 1048576 | bytes 6291456 | tf_op jit(solution)/shard_map/psum | solution.py:58
  353.1 4.5 convolution_convert_fusion.4
  361.4 2.7 copy.144
  364.1 2.5 fusion.279
  366.5 4.2 copy.145
  373.2 4.2 copy.146
  377.5 2.2 fusion.114
  380.4 13.6 %psum.51 = f32[4,2048]{1,0:T(4,128)S(1)} all-reduce(f32[4,2048]{1,0:T(4,128)S(1)} %fusion.9), channel_id=1, replica_groups=mesh['section'=2,'req'=32,'head'=4] {'head'}, use_global_device_ids=true, to_apply=%region_13.14 | all-reduce | flops 8192 | bytes 65536 | tf_op jit(solution)/shard_map/psum | solution.py:192
  403.2 4.5 convolution_convert_fusion.3
  430.1 17.8 %psum.52 = f32[4,2048]{1,0:T(4,128)} all-reduce(f32[4,2048]{1,0:T(4,128)} %fusion.7), channel_id=1, replica_groups=mesh['section'=2,'req'=32,'head'=4] {'head'}, use_global_device_ids=true, to_apply=%region_25.26 | all-reduce | flops 8192 | bytes 65536 | tf_op jit(solution)/shard_map/psum | solution.py:192
  459.8 4.5 convolution_convert_fusion.2
  484.3 2.7 fusion.33
  489.0 14.9 %psum.53 = f32[4,2048]{1,0:T(4,128)} all-reduce(f32[4,2048]{1,0:T(4,128)S(1)} %fusion.5), channel_id=1, replica_groups=mesh['section'=2,'req'=32,'head'=4] {'head'}, use_global_device_ids=true, to_apply=%region_37.38 | all-reduce | flops 8192 | bytes 65536 | tf_op jit(solution)/shard_map/psum | solution.py:192
  517.5 4.5 convolution_convert_fusion.1
  537.6 2.5 fusion.80
  540.3 3.4 fusion.31
  546.6 17.5 %psum.54 = f32[4,2048]{1,0:T(4,128)} all-reduce(f32[4,2048]{1,0:T(4,128)} %fusion.3), channel_id=1, replica_groups=mesh['section'=2,'req'=32,'head'=4] {'head'}, use_global_device_ids=true, to_apply=%region_49.50 | all-reduce | flops 8192 | bytes 65536 | tf_op jit(solution)/shard_map/psum | solution.py:192
  573.2 4.5 convolution_convert_fusion
  593.3 3.6 fusion.39
  598.6 3.4 fusion.26
  603.7 14.9 %psum.55 = f32[4,2048]{1,0:T(4,128)} all-reduce(f32[4,2048]{1,0:T(4,128)S(1)} %fusion.1), channel_id=1, replica_groups=mesh['section'=2,'req'=32,'head'=4] {'head'}, use_global_device_ids=true, to_apply=%region_61.62 | all-reduce | flops 8192 | bytes 65536 | tf_op jit(solution)/shard_map/psum | solution.py:192
  621.6 5.1 add_select_fusion
  (506 shorter events, 148.5 us)
Async XLA Ops:
  7.2 372.8 %copy-start = (bf16[1,512,2048]{2,1,0:T(8,128)(2,1)S(1)}, bf16[1,512,2048]{2,1,0:T(8,128)(2,1)}, u32[]{:S(2)}) copy-start(bf16[1,512,2048]{2,1,0:T(8,128)(2,1)} %param.24) | copy-start | bytes 6291460
  7.2 151.1 %all-reduce.3.cloned.1.call-start = ((), (), s32[]{:S(2)}) async-start(), calls=%async_computation.2 | async-start | bytes 8388608 | tf_op jit(solution)/shard_map/psum | solution.py:58
  69.3 24.5 %all-to-all-start = ((f32[1,128,4,4,128]{4,3,2,0,1:T(4,128)}), f32[1,128,4,4,128]{4,3,2,0,1:T(4,128)S(1)}, u32[]{:S(2)}, u32[]{:S(2)}) async-start(f32[1,128,4,4,128]{4,3,2,0,1:T(4,128)} %bitcast_select_fusion.1), calls=%async_computation | async-start | bytes 2097152 | tf_op jit(solution)/shard_map/all_to_all | solution.py:64
  80.8 6.8 %copy-start.22 = (bf16[1,4,4,2,512]{4,3,2,1,0:T(2,128)(2,1)S(1)}, bf16[1,4,4,2,512]{4,3,2,1,0:T(2,128)(2,1)}, u32[]{:S(2)}) copy-start(bf16[1,4,4,2,512]{4,3,2,1,0:T(2,128)(2,1)} %param.22) | copy-start | bytes 98308
  87.7 273.1 %copy-start.91 = (bf16[4,4,512]{2,1,0:T(4,128)(2,1)}, bf16[4,4,512]{2,1,0:T(4,128)(2,1)S(1)}, u32[]{:S(2)}) copy-start(bf16[4,4,512]{2,1,0:T(4,128)(2,1)S(1)} %get-tuple-element.17) | copy-start | bytes 49156
  87.7 292.0 %copy-start.86 = (bf16[4,4,512]{2,1,0:T(4,128)(2,1)}, bf16[4,4,512]{2,1,0:T(4,128)(2,1)S(1)}, u32[]{:S(2)}) copy-start(bf16[4,4,512]{2,1,0:T(4,128)(2,1)S(1)} %get-tuple-element.16) | copy-start | bytes 49156
  93.1 11.4 %copy-start.11 = (bf16[1,4,3,3,512]{4,1,3,2,0:T(4,128)(2,1)S(1)}, bf16[1,4,3,3,512]{4,1,3,2,0:T(4,128)(2,1)}, u32[]{:S(2)}) copy-start(bf16[1,4,3,3,512]{4,1,3,2,0:T(4,128)(2,1)} %param.21) | copy-start | bytes 110596
  93.1 11.4 %copy-start.79 = (f32[1,4,3,512]{3,1,2,0:T(4,128)S(1)}, f32[1,4,3,512]{3,1,2,0:T(4,128)}, u32[]{:S(2)}) copy-start(f32[1,4,3,512]{3,1,2,0:T(4,128)} %param.26) | copy-start | bytes 73732
  94.7 266.6 %all-to-all-start.1 = ((bf16[1,128,16,2,512]{4,2,3,0,1:T(8,128)(2,1)}), bf16[1,128,16,2,512]{4,2,3,0,1:T(8,128)(2,1)}, u32[]{:S(2)}, u32[]{:S(2)}) async-start(bf16[1,128,16,2,512]{4,2,3,0,1:T(8,128)(2,1)} %fusion), calls=%async_computation.1 | async-start | bytes 8388608 | tf_op jit(solution)/shard_map/all_to_all | solution.py:68
  117.9 235.2 %copy-start.12 = (f32[1,2048]{1,0:T(1,128)S(1)}, f32[1,2048]{1,0:T(1,128)}, u32[]{:S(2)}) copy-start(f32[1,2048]{1,0:T(1,128)} %param.27) | copy-start | bytes 24580
  361.3 46.4 %copy-start.8 = (bf16[4,3,3,512]{3,0,2,1:T(4,128)(2,1)}, bf16[4,3,3,512]{3,0,2,1:T(4,128)(2,1)S(1)}, u32[]{:S(2)}) copy-start(bf16[4,3,3,512]{3,0,2,1:T(4,128)(2,1)S(1)} %maximum_select_fusion) | copy-start | bytes 110596
  394.6 6.2 collective-permute-start
  409.0 16.0 %copy-start.29 = (f32[4,4,128]{2,1,0:T(4,128)S(1)}, f32[4,4,128]{2,1,0:T(4,128)}, u32[]{:S(2)}) copy-start(f32[4,4,128]{2,1,0:T(4,128)} %copy-done.28) | copy-start | bytes 24580
  409.0 16.0 %copy-start.34 = (f32[4,128,4]{1,2,0:T(4,128)S(1)}, f32[4,128,4]{1,2,0:T(4,128)}, u32[]{:S(2)}) copy-start(f32[4,128,4]{1,2,0:T(4,128)} %copy-done.33) | copy-start | bytes 24580
  409.8 17.5 %copy-start.63 = (f32[4,128,4]{1,2,0:T(4,128)}, f32[4,128,4]{1,2,0:T(4,128)S(1)}, u32[]{:S(2)}) copy-start(f32[4,128,4]{1,2,0:T(4,128)S(1)} %fusion.317) | copy-start | bytes 24580
  411.9 9.7 %copy-start.78 = (f32[4,1,512]{2,0,1:T(4,128)S(1)}, f32[4,1,512]{2,0,1:T(4,128)}, u32[]{:S(2)}) copy-start(f32[4,1,512]{2,0,1:T(4,128)} %get-tuple-element.97) | copy-start | bytes 24580
  427.4 20.5 %slice-start = ((bf16[4,3,3,512]{3,0,2,1:T(4,128)(2,1)}), bf16[4,2,3,512]{3,0,2,1:T(4,128)(2,1)S(1)}, s32[]{:S(2)}) async-start(bf16[4,3,3,512]{3,0,2,1:T(4,128)(2,1)} %copy-done.8), calls=%async_computation.3 | async-start | bytes 49152 | tf_op jit(solution)/shard_map/slice | solution.py:194
  427.4 20.5 %copy-start.24 = (bf16[4,1536]{1,0:T(4,128)(2,1)S(1)}, bf16[4,1536]{1,0:T(4,128)(2,1)}, u32[]{:S(2)}) copy-start(bf16[4,1536]{1,0:T(4,128)(2,1)} %copy-done.23) | copy-start | bytes 36868
  449.9 7.5 %collective-permute-start.1 = (bf16[4,2048]{1,0:T(4,128)(2,1)}, bf16[4,2048]{1,0:T(4,128)(2,1)}, u32[]{:S(2)}, u32[]{:S(2)}) collective-permute-start(bf16[4,2048]{1,0:T(4,128)(2,1)} %get-tuple-element.57), channel_id=1, source_target_pairs={{0,128},{1,129},{2,130},{3,131},{4,132},{5,133},{6,134},{7,135},{8... | collective-permute-start | bytes 49160 | tf_op jit(solution)/shard_map/ppermute | solution.py:14
  453.2 11.1 %copy-start.21 = (bf16[2,4,8,128]{3,2,0,1:T(8,128)(2,1)}, bf16[2,4,8,128]{3,2,0,1:T(8,128)(2,1)S(1)}, u32[]{:S(2)}) copy-start(bf16[2,4,8,128]{3,2,0,1:T(8,128)(2,1)S(1)} %broadcast_select_fusion.5) | copy-start | bytes 49156
  464.3 17.5 %copy-start.30 = (f32[4,4,128]{2,1,0:T(4,128)S(1)}, f32[4,4,128]{2,1,0:T(4,128)}, u32[]{:S(2)}) copy-start(f32[4,4,128]{2,1,0:T(4,128)} %copy-done.28) | copy-start | bytes 24580
  472.8 11.3 %copy-start.35 = (f32[4,128,4]{1,2,0:T(4,128)S(1)}, f32[4,128,4]{1,2,0:T(4,128)}, u32[]{:S(2)}) copy-start(f32[4,128,4]{1,2,0:T(4,128)} %copy-done.33) | copy-start | bytes 24580
  504.7 17.3 %copy-start.9 = (bf16[4,3,3,512]{3,0,2,1:T(4,128)(2,1)}, bf16[4,3,3,512]{3,0,2,1:T(4,128)(2,1)S(1)}, u32[]{:S(2)}) copy-start(bf16[4,3,3,512]{3,0,2,1:T(4,128)(2,1)S(1)} %maximum_select_fusion.2) | copy-start | bytes 110596
  506.1 8.9 %collective-permute-start.2 = (bf16[4,2048]{1,0:T(4,128)(2,1)}, bf16[4,2048]{1,0:T(4,128)(2,1)}, u32[]{:S(2)}, u32[]{:S(2)}) collective-permute-start(bf16[4,2048]{1,0:T(4,128)(2,1)} %get-tuple-element.51), channel_id=1, source_target_pairs={{0,128},{1,129},{2,130},{3,131},{4,132},{5,133},{6,134},{7,135},{8... | collective-permute-start | bytes 49160 | tf_op jit(solution)/shard_map/ppermute | solution.py:14
  543.9 20.2 %slice-start.1 = ((bf16[4,3,3,512]{3,0,2,1:T(4,128)(2,1)}), bf16[4,2,3,512]{3,0,2,1:T(4,128)(2,1)S(1)}, s32[]{:S(2)}) async-start(bf16[4,3,3,512]{3,0,2,1:T(4,128)(2,1)} %copy-done.9), calls=%async_computation.4 | async-start | bytes 49152 | tf_op jit(solution)/shard_map/slice | solution.py:194
  543.9 20.2 %copy-start.26 = (bf16[4,1536]{1,0:T(4,128)(2,1)S(1)}, bf16[4,1536]{1,0:T(4,128)(2,1)}, u32[]{:S(2)}) copy-start(bf16[4,1536]{1,0:T(4,128)(2,1)} %copy-done.25) | copy-start | bytes 36868
  565.6 6.7 %collective-permute-start.3 = (bf16[4,2048]{1,0:T(4,128)(2,1)S(1)}, bf16[4,2048]{1,0:T(4,128)(2,1)}, u32[]{:S(2)}, u32[]{:S(2)}) collective-permute-start(bf16[4,2048]{1,0:T(4,128)(2,1)S(1)} %get-tuple-element.45), channel_id=1, source_target_pairs={{0,128},{1,129},{2,130},{3,131},{4,132},{5,133},{6,134},{7,135},{8... | collective-permute-start | bytes 49160 | tf_op jit(solution)/shard_map/ppermute | solution.py:14
  577.7 9.4 %copy-start.80 = (pred[4,512]{1,0:T(4,128)(4,1)S(1)}, pred[4,512]{1,0:T(4,128)(4,1)}, u32[]{:S(2)}) copy-start(pred[4,512]{1,0:T(4,128)(4,1)} %iota_compare_fusion) | copy-start | bytes 6148
  582.8 9.9 %copy-start.77 = (f32[4,1,512]{2,0,1:T(4,128)S(1)}, f32[4,1,512]{2,0,1:T(4,128)}, u32[]{:S(2)}) copy-start(f32[4,1,512]{2,0,1:T(4,128)} %get-tuple-element.88) | copy-start | bytes 24580
  602.4 19.2 %copy-start.6 = (f32[1,4,32,4,4,128]{5,4,3,2,1,0:T(4,128)S(1)}, f32[1,4,32,4,4,128]{5,4,3,2,1,0:T(4,128)}, u32[]{:S(2)}) copy-start(f32[1,4,32,4,4,128]{5,4,3,2,1,0:T(4,128)} %copy.150) | copy-start | bytes 3145732
  603.0 18.5 %copy-start.58 = (f32[4,4,128]{2,1,0:T(4,128)S(1)}, f32[4,4,128]{2,1,0:T(4,128)}, u32[]{:S(2)}) copy-start(f32[4,4,128]{2,1,0:T(4,128)} %copy-done.55) | copy-start | bytes 24580
  603.0 18.5 %copy-start.61 = (f32[4,4,128]{2,1,0:T(4,128)S(1)}, f32[4,4,128]{2,1,0:T(4,128)}, u32[]{:S(2)}) copy-start(f32[4,4,128]{2,1,0:T(4,128)} %copy-done.59) | copy-start | bytes 24580
  (96 other events, 294.7 us)
Sparse Core Ops, SparseCore 0:
  63.8 94.3 all-reduce.2
